TPU v7x, 32 devices: a whole 2x2x4 slice. The times are simulated.
32 devices in a mesh: group: 2 (over y), ctx: 8 (over z, x), head: 2 (over core).
Axes of the slice: x: 2, y: 2, z: 4, core: 2. Of those that a mesh axis runs over, the one named last changes fastest.
Arguments:
- queries: bfloat16 [4096, 4096], P(('group', 'ctx'), 'head'), parts along dimension 0, may hold values from -7 to 7
- keys: bfloat16 [4096, 1024], P(('group', 'ctx'), 'head'), parts along dimension 0, may hold values from -4 to 4
- values: bfloat16 [4096, 1024], P(('group', 'ctx'), 'head'), parts along dimension 0, may hold values from -24 to 24
- doc_of_block: int32 [32], P('group'), parts along dimension 0, may hold values from 0 to 4, never falling along the last dimension, each value on 1 to 8 neighbouring positions
- out_weight: bfloat16 [4096, 4096], P('ctx', 'head'), may hold values from -0.09375 to 0.09375
Outputs:
- mixed: bfloat16 [4096, 4096], P(('group', 'ctx'), 'head'), parts along dimension 0
There are 2 independent parts, one for each index of `group`. A program takes and returns all parts, laid end to end along the dimension named above; an argument that names none is the same for every part. Nothing has to cross between parts.
Inputs may be any that keep to these rules, and one draw needn't show every extreme that they name: `doc_of_block`: blocks of one document are consecutive, and a document covers at most 8 blocks.
All inputs are finite; a program needn't handle non-finite values.
Results may differ from a plain program's by a relative error of at most 0.006.
Values may be sent and summed in bfloat16 or wider, within the bound.
No kernel may reach another device: no remote copies, remote signals or barrier semaphores. Data moves between devices by JAX's collectives and lax.ppermute only.
A program may use at most 64 MiB of HBM per device.

v0:
```python
import math
import jax
import jax.numpy as jnp
from jax import lax
from jax.sharding import PartitionSpec as P

HEAD_SIZE = 128
BLOCK_TOKENS = 128


def passed_along(array, axis, by):
    peers = lax.axis_size(axis)
    pairs = [(i, i + by) for i in range(peers) if 0 <= i + by < peers]
    return lax.ppermute(array, axis, pairs)


def lookup_docs(positions, doc_of_block):
    block_ids = jnp.floor_divide(positions, BLOCK_TOKENS)
    table_ids = jnp.arange(doc_of_block.shape[0], dtype=jnp.int32)
    matches = block_ids[:, None] == table_ids[None, :]
    return jnp.max(jnp.where(matches, doc_of_block[None, :], -1), axis=1)


def update(state_now, query_head_rows, key_piece, value_piece, visible):
    running_max, summed, totals = state_now
    rows_here = key_piece.shape[0]
    kv_heads = query_head_rows.shape[1]
    key_head_rows = key_piece.reshape(rows_here, kv_heads, HEAD_SIZE)
    value_head_rows = value_piece.reshape(rows_here, kv_heads, HEAD_SIZE)
    score_scale = 1.0 / math.sqrt(HEAD_SIZE)
    scores = (
        jnp.einsum(
            "qhgd,khd->hgqk", query_head_rows, key_head_rows, preferred_element_type=jnp.float32
        )
        * score_scale
    )
    scores = jnp.where(visible, scores, -1e30)
    new_max = jnp.maximum(running_max, jnp.max(scores, axis=-1))
    weights = jnp.where(visible, jnp.exp(scores - new_max[..., None]), 0.0)
    rescale = jnp.exp(running_max - new_max)
    products = jnp.einsum(
        "hgqk,khd->hgqd",
        weights.astype(jnp.bfloat16),
        value_head_rows,
        preferred_element_type=jnp.float32,
    )
    summed = summed * rescale[..., None] + products
    totals = totals * rescale + jnp.sum(weights, axis=-1)
    return (new_max, summed, totals)


def fresh_state(kv_heads, group_width, rows_here):
    return (
        jnp.full((kv_heads, group_width, rows_here), -1e30, jnp.float32),
        jnp.zeros((kv_heads, group_width, rows_here, HEAD_SIZE), jnp.float32),
        jnp.zeros((kv_heads, group_width, rows_here), jnp.float32),
    )


def finish(state_now, rows_here, q_heads):
    running_max, summed, totals = state_now
    attended = summed / totals[..., None]
    return (
        jnp.transpose(attended, (2, 0, 1, 3))
        .reshape(rows_here, q_heads * HEAD_SIZE)
        .astype(jnp.bfloat16)
    )


def per_device(queries, keys, values, doc_of_block, out_weight):
    tok_rows = queries.shape[0]
    kv_heads = keys.shape[1] // HEAD_SIZE
    q_heads = queries.shape[1] // HEAD_SIZE
    group_width = q_heads // kv_heads
    ctx_count = lax.axis_size("ctx")
    reach_devs = min(8, ctx_count // 2)
    ctx_index = lax.axis_index("ctx")
    query_start = ctx_index * tok_rows
    query_pos = query_start + jnp.arange(tok_rows, dtype=jnp.int32)
    query_doc = lookup_docs(query_pos, doc_of_block)
    query_head_rows = queries.reshape(tok_rows, kv_heads, group_width, HEAD_SIZE)

    def attend(state_now, key_piece, value_piece, key_start):
        key_pos = key_start + jnp.arange(key_piece.shape[0], dtype=jnp.int32)
        key_doc = lookup_docs(key_pos, doc_of_block)
        visible = (key_doc[None, :] == query_doc[:, None]) & (
            key_pos[None, :] <= query_pos[:, None]
        )
        return update(state_now, query_head_rows, key_piece, value_piece, visible)

    initial_state = fresh_state(kv_heads, group_width, tok_rows)
    state_now = attend(initial_state, keys, values, query_start)
    for distance in range(1, reach_devs + 1):
        prior_keys, prior_values = passed_along((keys, values), "ctx", distance)
        state_now = attend(state_now, prior_keys, prior_values, query_start - distance * tok_rows)
    attended = finish(state_now, tok_rows, q_heads)
    features = lax.all_gather(attended, "head", axis=1, tiled=True)
    mixed = jnp.dot(
        features,
        lax.all_gather(out_weight, "ctx", axis=0, tiled=True),
        preferred_element_type=jnp.float32,
    )
    return mixed.astype(jnp.bfloat16)


def solution(mesh):
    return jax.shard_map(
        per_device,
        mesh=mesh,
        in_specs=(
            P(("group", "ctx"), "head"),
            P(("group", "ctx"), "head"),
            P(("group", "ctx"), "head"),
            P("group"),
            P("ctx", "head"),
        ),
        out_specs=P(("group", "ctx"), "head"),
        check_vma=False,
    )
```

profile of v0, /device:TPU:0, one launch (start us, length us, event | category | flops | bytes accessed | tf_op | source)
XLA Modules:
  0.0 352.3 jit_solution(2587613839477615480)
XLA Ops:
  6.5 1.1 copy.50
  7.6 6.0 %collective-permute-start.6 = (bf16[256,512]{0,1:T(8,128)(2,1)S(1)}, bf16[256,512]{0,1:T(8,128)(2,1)S(1)}, u32[]{:S(2)}, u32[]{:S(2)}) collective-permute-start(bf16[256,512]{0,1:T(8,128)(2,1)S(1)} %copy.50), channel_id=1, source_target_pairs={{0,8},{2,10},{4,12},{6,14},{1,9},{3,11},{5,13},{7,15},{16,24},{18,... | collective-permute-start | bytes 786440 | tf_op jit(solution)/shard_map/ppermute | solution.py:14
  13.6 4.4 %collective-permute-start.4 = (bf16[256,512]{0,1:T(8,128)(2,1)S(1)}, bf16[256,512]{0,1:T(8,128)(2,1)S(1)}, u32[]{:S(2)}, u32[]{:S(2)}) collective-permute-start(bf16[256,512]{0,1:T(8,128)(2,1)S(1)} %copy.50), channel_id=1, source_target_pairs={{0,6},{2,8},{4,10},{6,12},{8,14},{1,7},{3,9},{5,11},{7,13},{9,15},... | collective-permute-start | bytes 786440 | tf_op jit(solution)/shard_map/ppermute | solution.py:14
  18.0 1.3 collective-permute-start.2
  19.4 3.1 collective-permute-start
  22.5 2.7 collective-permute-start.1
  26.2 1.9 copy.87
  28.2 1.8 reshape.265
  32.3 2.6 collective-permute-start.3
  34.9 2.9 fusion.4
  37.8 2.6 collective-permute-start.5
  40.4 3.0 fusion.3
  43.4 4.1 %collective-permute-start.7 = (bf16[256,512]{1,0:T(8,128)(2,1)S(1)}, bf16[256,512]{1,0:T(8,128)(2,1)S(1)}, u32[]{:S(2)}, u32[]{:S(2)}) collective-permute-start(bf16[256,512]{1,0:T(8,128)(2,1)S(1)} %copy-done.4), channel_id=1, source_target_pairs={{0,8},{2,10},{4,12},{6,14},{1,9},{3,11},{5,13},{7,15},{16,24},{18,... | collective-permute-start | bytes 786440 | tf_op jit(solution)/shard_map/ppermute | solution.py:14
  47.5 3.0 fusion.2
  51.6 1.0 fusion.5
  52.6 2.5 fusion.23
  56.4 4.9 %fusion.21 = f32[4,4,256,128]{2,3,1,0:T(8,128)} fusion(bf16[256,4,128,1]{0,2,3,1:T(8,128)(2,1)S(1)} %bitcast.249, f32[4,256,256,4]{2,1,3,0:T(8,128)} %copy-done.3, f32[4,4,256]{2,1,0:T(4,128)S(1)} %get-tuple-element.17, pred[256,256]{0,1:T(8,128)(4,1)S(1)} %get-tuple-element.22), kind=kOutput, calls=%fused_computation.29 | convolution fusion | flops 273678336 | bytes 6635520 | tf_op jit(solution)/shard_map/hgqk,khd->hgqd/dot_general | solution.py:41
  62.3 1.1 copy.58
  63.4 4.9 %fusion.19 = f32[4,4,256,128]{2,3,1,0:T(8,128)} fusion(bf16[256,4,128,1]{0,2,3,1:T(8,128)(2,1)S(1)} %bitcast.250, f32[4,256,256,4]{2,1,3,0:T(8,128)} %get-tuple-element.31, f32[4,4,256]{2,1,0:T(4,128)S(1)} %get-tuple-element.16, pred[256,256]{0,1:T(8,128)(4,1)S(1)} %get-tuple-element.24), kind=kOutput, calls=%fused_computation.28 | convolution fusion | flops 273678336 | bytes 6635520 | tf_op jit(solution)/shard_map/hgqk,khd->hgqd/dot_general | solution.py:41
  69.5 4.9 %fusion.17 = f32[4,4,256,128]{2,3,1,0:T(8,128)} fusion(bf16[256,4,128,1]{0,2,3,1:T(8,128)(2,1)S(1)} %bitcast.251, f32[4,256,256,4]{2,1,3,0:T(8,128)} %get-tuple-element.29, f32[4,4,256]{2,1,0:T(4,128)S(1)} %get-tuple-element.15, pred[256,256]{0,1:T(8,128)(4,1)S(1)} %get-tuple-element.23), kind=kOutput, calls=%fused_computation.27 | convolution fusion | flops 273678336 | bytes 6635520 | tf_op jit(solution)/shard_map/hgqk,khd->hgqd/dot_general | solution.py:41
  75.8 7.4 %fusion.26 = bf16[256,4,4,128]{0,3,2,1:T(8,128)(2,1)} fusion(f32[4,4,256,128]{2,3,1,0:T(8,128)} %fusion.17, f32[4,4,256,128]{2,3,1,0:T(8,128)} %fusion.19, f32[4,4,256,128]{2,3,1,0:T(8,128)} %fusion.21, f32[4,4,256,128]{2,3,1,0:T(8,128)} %fusion.23, f32[256,4,4]{0,2,1:T(4,128)S(1)} %get-tuple-element.10, f32[256,4,4]{0,2,1:T(4,128)S(1)} %get-tuple-element.13, ...), kind=kOutput, calls=%fused_computation.33 | convolution fusion | flops 279445504 | bytes 14073856 | tf_op jit(solution)/shard_map/hgqk,khd->hgqd/dot_general | solution.py:41
  84.0 19.0 %all-gather.3.cloned.1.call-done = bf16[256,4096]{0,1:T(8,128)(2,1)} async-done(((bf16[256,2048]{0,1:T(8,128)(2,1)}), bf16[256,4096]{0,1:T(8,128)(2,1)}) %all-gather.3.cloned.1.call-update) | async-done | bytes 2097168 | tf_op jit(solution)/shard_map/all_gather | solution.py:97
  103.0 230.6 %all-gather.5.cloned.1.call-done = bf16[4096,2048]{1,0:T(8,128)(2,1)} async-done(((bf16[512,2048]{1,0:T(8,128)(2,1)}), bf16[4096,2048]{1,0:T(8,128)(2,1)}) %all-gather.5.cloned.1.call-update) | async-done | bytes 16777232 | tf_op jit(solution)/shard_map/all_gather | solution.py:100
  333.6 11.9 %convolution_convert_fusion = bf16[256,2048]{1,0:T(8,128)(2,1)} fusion(bf16[256,4096]{0,1:T(8,128)(2,1)} %all-gather.3.cloned.1.call-done, bf16[4096,2048]{1,0:T(8,128)(2,1)} %all-gather.5.cloned.1.call-done), kind=kOutput, calls=%fused_computation.25 | convolution fusion | flops 4295491584 | bytes 19922944 | tf_op jit(solution)/shard_map/dot_general | solution.py:98
  (43 shorter events, 10.0 us)
Async XLA Ops:
  6.5 96.4 %all-gather.3.cloned.1.call-start = ((), (), s32[]{:S(2)}) async-start(), calls=%async_computation | async-start | bytes 3145728 | tf_op jit(solution)/shard_map/all_gather | solution.py:97
  7.6 24.6 %collective-permute-start.6 = (bf16[256,512]{0,1:T(8,128)(2,1)S(1)}, bf16[256,512]{0,1:T(8,128)(2,1)S(1)}, u32[]{:S(2)}, u32[]{:S(2)}) collective-permute-start(bf16[256,512]{0,1:T(8,128)(2,1)S(1)} %copy.50), channel_id=1, source_target_pairs={{0,8},{2,10},{4,12},{6,14},{1,9},{3,11},{5,13},{7,15},{16,24},{18,... | collective-permute-start | bytes 786440 | tf_op jit(solution)/shard_map/ppermute | solution.py:14
  13.6 24.2 %collective-permute-start.4 = (bf16[256,512]{0,1:T(8,128)(2,1)S(1)}, bf16[256,512]{0,1:T(8,128)(2,1)S(1)}, u32[]{:S(2)}, u32[]{:S(2)}) collective-permute-start(bf16[256,512]{0,1:T(8,128)(2,1)S(1)} %copy.50), channel_id=1, source_target_pairs={{0,6},{2,8},{4,10},{6,12},{8,14},{1,7},{3,9},{5,11},{7,13},{9,15},... | collective-permute-start | bytes 786440 | tf_op jit(solution)/shard_map/ppermute | solution.py:14
  18.0 25.4 %collective-permute-start.2 = (bf16[256,512]{0,1:T(8,128)(2,1)S(1)}, bf16[256,512]{0,1:T(8,128)(2,1)S(1)}, u32[]{:S(2)}, u32[]{:S(2)}) collective-permute-start(bf16[256,512]{0,1:T(8,128)(2,1)S(1)} %copy.50), channel_id=1, source_target_pairs={{0,4},{2,6},{4,8},{6,10},{8,12},{10,14},{1,5},{3,7},{5,9},{7,11},{... | collective-permute-start | bytes 786440 | tf_op jit(solution)/shard_map/ppermute | solution.py:14
  19.4 31.1 %collective-permute-start = (bf16[256,512]{0,1:T(8,128)(2,1)S(1)}, bf16[256,512]{0,1:T(8,128)(2,1)S(1)}, u32[]{:S(2)}, u32[]{:S(2)}) collective-permute-start(bf16[256,512]{0,1:T(8,128)(2,1)S(1)} %copy.50), channel_id=1, source_target_pairs={{0,2},{2,4},{4,6},{6,8},{8,10},{10,12},{12,14},{1,3},{3,5},{5,7},{... | collective-permute-start | bytes 786440 | tf_op jit(solution)/shard_map/ppermute | solution.py:14
  22.5 33.7 %collective-permute-start.1 = (bf16[256,512]{1,0:T(8,128)(2,1)}, bf16[256,512]{1,0:T(8,128)(2,1)S(1)}, u32[]{:S(2)}, u32[]{:S(2)}) collective-permute-start(bf16[256,512]{1,0:T(8,128)(2,1)} %param.7), channel_id=1, source_target_pairs={{0,2},{2,4},{4,6},{6,8},{8,10},{10,12},{12,14},{1,3},{3,5},{5,7},{... | collective-permute-start | bytes 786440 | tf_op jit(solution)/shard_map/ppermute | solution.py:14
  26.2 6.1 %copy-start.4 = (bf16[256,512]{1,0:T(8,128)(2,1)S(1)}, bf16[256,512]{1,0:T(8,128)(2,1)}, u32[]{:S(2)}) copy-start(bf16[256,512]{1,0:T(8,128)(2,1)} %param.7) | copy-start | bytes 786436
  32.3 30.0 %collective-permute-start.3 = (bf16[256,512]{1,0:T(8,128)(2,1)S(1)}, bf16[256,512]{1,0:T(8,128)(2,1)}, u32[]{:S(2)}, u32[]{:S(2)}) collective-permute-start(bf16[256,512]{1,0:T(8,128)(2,1)S(1)} %copy-done.4), channel_id=1, source_target_pairs={{0,4},{2,6},{4,8},{6,10},{8,12},{10,14},{1,5},{3,7},{5,9},{7,11},{... | collective-permute-start | bytes 786440 | tf_op jit(solution)/shard_map/ppermute | solution.py:14
  37.8 31.5 %collective-permute-start.5 = (bf16[256,512]{1,0:T(8,128)(2,1)S(1)}, bf16[256,512]{1,0:T(8,128)(2,1)S(1)}, u32[]{:S(2)}, u32[]{:S(2)}) collective-permute-start(bf16[256,512]{1,0:T(8,128)(2,1)S(1)} %copy-done.4), channel_id=1, source_target_pairs={{0,6},{2,8},{4,10},{6,12},{8,14},{1,7},{3,9},{5,11},{7,13},{9,15},... | collective-permute-start | bytes 786440 | tf_op jit(solution)/shard_map/ppermute | solution.py:14
  43.4 32.0 %collective-permute-start.7 = (bf16[256,512]{1,0:T(8,128)(2,1)S(1)}, bf16[256,512]{1,0:T(8,128)(2,1)S(1)}, u32[]{:S(2)}, u32[]{:S(2)}) collective-permute-start(bf16[256,512]{1,0:T(8,128)(2,1)S(1)} %copy-done.4), channel_id=1, source_target_pairs={{0,8},{2,10},{4,12},{6,14},{1,9},{3,11},{5,13},{7,15},{16,24},{18,... | collective-permute-start | bytes 786440 | tf_op jit(solution)/shard_map/ppermute | solution.py:14
  50.5 2.1 copy-start.5
  51.5 3.6 %copy-start.3 = (f32[4,256,256,4]{2,1,3,0:T(8,128)}, f32[4,256,256,4]{2,1,3,0:T(8,128)S(1)}, u32[]{:S(2)}) copy-start(f32[4,256,256,4]{2,1,3,0:T(8,128)S(1)} %get-tuple-element.33) | copy-start | bytes 12582916
  56.4 4.9 %copy-start.2 = (f32[4,256,256,4]{2,1,3,0:T(8,128)S(1)}, f32[4,256,256,4]{2,1,3,0:T(8,128)}, u32[]{:S(2)}) copy-start(f32[4,256,256,4]{2,1,3,0:T(8,128)} %get-tuple-element.31) | copy-start | bytes 12582916
  63.4 4.9 %copy-start.1 = (f32[4,256,256,4]{2,1,3,0:T(8,128)S(1)}, f32[4,256,256,4]{2,1,3,0:T(8,128)}, u32[]{:S(2)}) copy-start(f32[4,256,256,4]{2,1,3,0:T(8,128)} %get-tuple-element.29) | copy-start | bytes 12582916
  69.5 4.9 %copy-start = (f32[4,256,256,4]{2,1,3,0:T(8,128)S(1)}, f32[4,256,256,4]{2,1,3,0:T(8,128)}, u32[]{:S(2)}) copy-start(f32[4,256,256,4]{2,1,3,0:T(8,128)} %get-tuple-element.27) | copy-start | bytes 12582916
  83.2 250.4 %all-gather.5.cloned.1.call-start = ((), (), s32[]{:S(2)}) async-start(), calls=%async_computation.1 | async-start | bytes 18874368 | tf_op jit(solution)/shard_map/all_gather | solution.py:100
Sparse Core Ops, SparseCore 0:
  83.3 19.5 all-gather.2
  105.1 228.4 all-gather.4
where the time goes:
time: 353 us; the launch traced here: 352 us
  waiting for transfers between devices  250 us (71%)
  matrix products  47.2 us (13%)
  starting transfers between devices  26.9 us (8%)
  between operations  13.7 us (4%)
  local copies, waits for them, and re-layouts  7.47 us (2%)
  other arithmetic  6.66 us (2%)
    all_gather x1, waiting for transfers between devices, per_device(): lax.all_gather(out_weight, 'ctx', axis=0, tiled=True)  231 us
    ppermute x8, starting transfers between devices, passed_along(): return lax.ppermute(array, axis, pairs)  26.9 us
    dot_general x5, matrix products, update(): jnp.einsum('hgqk,khd->hgqd', weights.astype(jnp.bfloat16), value_head_row...  24.5 us
    all_gather x1, waiting for transfers between devices, per_device(): features = lax.all_gather(attended, 'head', axis=1, tiled=True)  19 us
    dot_general x1, matrix products, per_device(): jnp.dot(features, lax.all_gather(out_weight, 'ctx', axis=0, tiled=True),...  11.9 us
    dot_general x5, matrix products, update(): jnp.einsum('qhgd,khd->hgqk', query_head_rows, key_head_rows, preferred_el...  10.8 us
  transfers between devices with their start and end apart: 10, of which 2 were waited for; matrix products, arithmetic and copies ran while one was open for 12% of the time, Pallas kernels for 0%

commit v1 on v0

--- a/solution.py
+++ b/solution.py
@@ -6,6 +6,28 @@
 
 HEAD_SIZE = 128
 BLOCK_TOKENS = 128
+
+
+def laid_out(blocks, dim):
+    shape = list(blocks.shape[1:])
+    shape[dim] *= blocks.shape[0]
+    return jnp.moveaxis(blocks, 0, dim).reshape(shape)
+
+
+def collect(x, axis, dim):
+    size = lax.axis_size(axis)
+    pairs = [(i, (i + 1) % size) for i in range(size)]
+    back = [(b, a) for a, b in pairs]
+    lower, upper = ([], [])
+    for turn in range(size - 1):
+        if turn % 2 == 0:
+            lower.append(lax.ppermute(lower[-1] if lower else x, axis, pairs))
+        else:
+            upper.append(lax.ppermute(upper[-1] if upper else x, axis, back))
+    parts = jnp.stack([*lower[::-1], x, *upper])
+    shift = lax.axis_index(axis) - len(lower)
+    parts = parts[(jnp.arange(size) - shift) % size]
+    return laid_out(parts, dim)
 
 
 def passed_along(array, axis, by):
@@ -95,11 +117,7 @@
         state_now = attend(state_now, prior_keys, prior_values, query_start - distance * tok_rows)
     attended = finish(state_now, tok_rows, q_heads)
     features = lax.all_gather(attended, "head", axis=1, tiled=True)
-    mixed = jnp.dot(
-        features,
-        lax.all_gather(out_weight, "ctx", axis=0, tiled=True),
-        preferred_element_type=jnp.float32,
-    )
+    mixed = jnp.dot(features, collect(out_weight, "ctx", 0), preferred_element_type=jnp.float32)
     return mixed.astype(jnp.bfloat16)
 
 

time: 353 us -> 441 us (1.25); the launches traced: 352 us -> 433 us
  starting transfers between devices: 26.9 us -> 73.6 us
  local copies, waits for them, and re-layouts: 7.47 us -> 44.4 us
  other arithmetic: 6.66 us -> 21.1 us
  matrix products: 47.2 us -> 34.8 us
  waiting for transfers between devices: 250 us -> 245 us
    all_gather x1 -> x0, waiting for transfers between devices: 231 us -> none  [per_device(): lax.all_gather(out_weight, 'ctx', axis=0, tiled=True)]
    ppermute x0 -> x7, waiting for transfers between devices: none -> 219 us  [the longest x3 110 us: collect(): upper.append(lax.ppermute(upper[-1] if upper else x, axis, back))]
    ppermute x8, starting transfers between devices: 26.9 us -> 55.7 us  [passed_along(): return lax.ppermute(array, axis, pairs)]
    ppermute x8, waiting for transfers between devices: 0.02 us -> 26.1 us  [passed_along(): return lax.ppermute(array, axis, pairs)]
    gather x0 -> x3, local copies, waits for them, and re-layouts: none -> 22.6 us  [collect(): parts = parts[(jnp.arange(size) - shift) % size]]
    all_gather x1, waiting for transfers between devices: 19 us -> 0.01 us  [per_device(): features = lax.all_gather(attended, 'head', axis=1, tiled=True)]
    ppermute x0 -> x7, starting transfers between devices: none -> 17.9 us  [the longest x4 10.3 us: collect(): lower.append(lax.ppermute(lower[-1] if lower else x, axis, pairs))]
    unnamed x0 -> x1, other arithmetic: none -> 13.8 us
  transfers between devices with their start and end apart: 10 -> 16, of which waited for: 2 -> 5; matrix products, arithmetic and copies ran while one was open for 12% -> 20% of each run, Pallas kernels for 0% -> 0%
where the time goes in v1:
time: 441 us; the launch traced here: 433 us
  waiting for transfers between devices  245 us (56%)
  starting transfers between devices  73.6 us (17%)
  local copies, waits for them, and re-layouts  44.4 us (10%)
  matrix products  34.8 us (8%)
  other arithmetic  21.1 us (5%)
  between operations  13.8 us (3%)
    ppermute x3, waiting for transfers between devices, collect(): upper.append(lax.ppermute(upper[-1] if upper else x, axis, back))  110 us
    ppermute x4, waiting for transfers between devices, collect(): lower.append(lax.ppermute(lower[-1] if lower else x, axis, pairs))  109 us
    ppermute x8, starting transfers between devices, passed_along(): return lax.ppermute(array, axis, pairs)  55.7 us
    ppermute x8, waiting for transfers between devices, passed_along(): return lax.ppermute(array, axis, pairs)  26.1 us
    gather x3, local copies, waits for them, and re-layouts, collect(): parts = parts[(jnp.arange(size) - shift) % size]  22.6 us
    unnamed x1, other arithmetic  13.8 us
    unnamed x36, local copies, waits for them, and re-layouts  13 us
    dot_general x5, matrix products, update(): jnp.einsum('hgqk,khd->hgqd', weights.astype(jnp.bfloat16), value_head_row...  12.8 us
  transfers between devices with their start and end apart: 16, of which 5 were waited for; matrix products, arithmetic and copies ran while one was open for 20% of the time, Pallas kernels for 0%

profile of v1, /device:TPU:0, one launch (start us, length us, event | category | flops | bytes accessed | tf_op | source)
XLA Modules:
  0.0 432.6 jit_solution(17743669794512715866)
XLA Ops:
  6.5 3.0 collective-permute-start.8
  11.3 4.5 %collective-permute-start.6 = (bf16[256,512]{0,1:T(8,128)(2,1)}, bf16[256,512]{0,1:T(8,128)(2,1)S(1)}, u32[]{:S(2)}, u32[]{:S(2)}) collective-permute-start(bf16[256,512]{0,1:T(8,128)(2,1)} %copy.50), channel_id=1, source_target_pairs={{0,8},{2,10},{4,12},{6,14},{1,9},{3,11},{5,13},{7,15},{16,24},{18,... | collective-permute-start | bytes 786440 | tf_op jit(solution)/shard_map/ppermute | solution.py:36
  15.8 2.9 collective-permute-start.4
  18.7 2.6 collective-permute-start.2
  21.3 3.3 collective-permute-start.1
  31.3 2.9 fusion
  34.2 26.1 %collective-permute-done.1 = bf16[256,512]{1,0:T(8,128)(2,1)S(1)} collective-permute-done((bf16[256,512]{1,0:T(8,128)(2,1)}, bf16[256,512]{1,0:T(8,128)(2,1)S(1)}, u32[]{:S(2)}, u32[]{:S(2)}) %collective-permute-start.1) | collective-permute-done | bytes 262176 | tf_op jit(solution)/shard_map/ppermute | solution.py:36
  60.3 21.1 %collective-permute-start = (bf16[256,512]{0,1:T(8,128)(2,1)}, bf16[256,512]{0,1:T(8,128)(2,1)}, u32[]{:S(2)}, u32[]{:S(2)}) collective-permute-start(bf16[256,512]{0,1:T(8,128)(2,1)} %copy.50), channel_id=1, source_target_pairs={{0,2},{2,4},{4,6},{6,8},{8,10},{10,12},{12,14},{1,3},{3,5},{5,7},{... | collective-permute-start | bytes 786440 | tf_op jit(solution)/shard_map/ppermute | solution.py:36
  82.3 14.7 %collective-permute-start.3 = (bf16[256,512]{1,0:T(8,128)(2,1)}, bf16[256,512]{1,0:T(8,128)(2,1)}, u32[]{:S(2)}, u32[]{:S(2)}) collective-permute-start(bf16[256,512]{1,0:T(8,128)(2,1)} %param.7), channel_id=1, source_target_pairs={{0,4},{2,6},{4,8},{6,10},{8,12},{10,14},{1,5},{3,7},{5,9},{7,11},{... | collective-permute-start | bytes 786440 | tf_op jit(solution)/shard_map/ppermute | solution.py:36
  97.0 3.3 collective-permute-start.9
  105.5 4.5 %collective-permute-start.7 = (bf16[256,512]{1,0:T(8,128)(2,1)}, bf16[256,512]{1,0:T(8,128)(2,1)}, u32[]{:S(2)}, u32[]{:S(2)}) collective-permute-start(bf16[256,512]{1,0:T(8,128)(2,1)} %param.7), channel_id=1, source_target_pairs={{0,8},{2,10},{4,12},{6,14},{1,9},{3,11},{5,13},{7,15},{16,24},{18,... | collective-permute-start | bytes 786440 | tf_op jit(solution)/shard_map/ppermute | solution.py:36
  115.4 73.6 %collective-permute-done.9 = bf16[512,2048]{1,0:T(8,128)(2,1)S(1)} collective-permute-done((bf16[512,2048]{1,0:T(8,128)(2,1)}, bf16[512,2048]{1,0:T(8,128)(2,1)S(1)}, u32[]{:S(2)}, u32[]{:S(2)}) %collective-permute-start.9) | collective-permute-done | bytes 2097184 | tf_op jit(solution)/shard_map/ppermute | solution.py:24
  194.6 2.5 fusion.23
  202.1 34.9 %collective-permute-done.10 = bf16[512,2048]{1,0:T(8,128)(2,1)} collective-permute-done((bf16[512,2048]{1,0:T(8,128)(2,1)S(1)}, bf16[512,2048]{1,0:T(8,128)(2,1)}, u32[]{:S(2)}, u32[]{:S(2)}) %collective-permute-start.10) | collective-permute-done | bytes 2097184 | tf_op jit(solution)/shard_map/ppermute | solution.py:24
  243.1 3.5 fusion.19
  249.5 2.9 fusion.26
  252.5 74.3 %collective-permute-done.13 = bf16[512,2048]{1,0:T(8,128)(2,1)} collective-permute-done((bf16[512,2048]{1,0:T(8,128)(2,1)}, bf16[512,2048]{1,0:T(8,128)(2,1)}, u32[]{:S(2)}, u32[]{:S(2)}) %collective-permute-start.13) | collective-permute-done | bytes 2097184 | tf_op jit(solution)/shard_map/ppermute | solution.py:26
  326.8 5.2 %collective-permute-start.14 = (bf16[512,2048]{1,0:T(8,128)(2,1)}, bf16[512,2048]{1,0:T(8,128)(2,1)S(1)}, u32[]{:S(2)}, u32[]{:S(2)}) collective-permute-start(bf16[512,2048]{1,0:T(8,128)(2,1)} %collective-permute-done.13), channel_id=1, source_target_pairs={{2,0},{4,2},{6,4},{8,6},{10,8},{12,10},{14,12},{0,14},{3,1},{5,3},... | collective-permute-start | bytes 6291464 | tf_op jit(solution)/shard_map/ppermute | solution.py:26
  341.5 35.9 %collective-permute-done.14 = bf16[512,2048]{1,0:T(8,128)(2,1)S(1)} collective-permute-done((bf16[512,2048]{1,0:T(8,128)(2,1)}, bf16[512,2048]{1,0:T(8,128)(2,1)S(1)}, u32[]{:S(2)}, u32[]{:S(2)}) %collective-permute-start.14) | collective-permute-done | bytes 2097184 | tf_op jit(solution)/shard_map/ppermute | solution.py:26
  377.5 6.2 %fusion.98 = (bf16[8,512,1024]{2,1,0:T(8,128)(2,1)}, bf16[8,512,1024]{2,1,0:T(8,128)(2,1)}) fusion(bf16[8,512,2048]{2,1,0:T(8,128)(2,1)S(1)} %bitcast_dynamic-update-slice_fusion), kind=kLoop, calls=%fused_computation.175 | loop fusion | bytes 33554432 | tf_op jit(solution)/shard_map/gather | solution.py:29
  383.7 8.2 %gather_fusion = bf16[8,512,1024]{2,1,0:T(8,128)(2,1)} fusion(bf16[8,512,1024]{2,1,0:T(8,128)(2,1)} %get-tuple-element.18, s32[1024]{0:T(1024)} %pad_clamp_fusion), kind=kCustom, calls=%fused_computation | custom fusion | bytes 16777248 | tf_op jit(solution)/shard_map/gather | solution.py:29
  391.9 8.2 %gather_fusion.1 = bf16[8,512,1024]{2,1,0:T(8,128)(2,1)} fusion(bf16[8,512,1024]{2,1,0:T(8,128)(2,1)} %get-tuple-element.19, s32[1024]{0:T(1024)} %pad_clamp_fusion), kind=kCustom, calls=%fused_computation.1 | custom fusion | bytes 16777248 | tf_op jit(solution)/shard_map/gather | solution.py:29
  400.1 13.8 %pad_maximum_fusion = bf16[8,512,2048]{2,1,0:T(8,128)(2,1)} fusion(bf16[8,512,1024]{2,1,0:T(8,128)(2,1)} %gather_fusion.1, bf16[8,512,1024]{2,1,0:T(8,128)(2,1)} %gather_fusion), kind=kLoop, calls=%fused_computation.2 | loop fusion | flops 33554432 | bytes 33554432
  413.9 11.9 %convolution_convert_fusion = bf16[256,2048]{1,0:T(8,128)(2,1)} fusion(bf16[256,4096]{0,1:T(8,128)(2,1)} %all-gather.2.cloned.1.call-done, bf16[4096,2048]{1,0:T(8,128)(2,1)} %bitcast.260), kind=kOutput, calls=%fused_computation.28 | convolution fusion | flops 4295491584 | bytes 19922944 | tf_op jit(solution)/shard_map/dot_general | solution.py:120
  (84 shorter events, 48.7 us)
Async XLA Ops:
  6.5 407.4 %all-gather.2.cloned.1.call-start = ((), (), s32[]{:S(2)}) async-start(), calls=%async_computation | async-start | bytes 3145728 | tf_op jit(solution)/shard_map/all_gather | solution.py:119
  6.5 90.4 %collective-permute-start.8 = (bf16[512,2048]{1,0:T(8,128)(2,1)}, bf16[512,2048]{1,0:T(8,128)(2,1)}, u32[]{:S(2)}, u32[]{:S(2)}) collective-permute-start(bf16[512,2048]{1,0:T(8,128)(2,1)} %param.9), channel_id=1, source_target_pairs={{0,2},{2,4},{4,6},{6,8},{8,10},{10,12},{12,14},{14,0},{1,3},{3,5},... | collective-permute-start | bytes 6291464 | tf_op jit(solution)/shard_map/ppermute | solution.py:24
  11.3 71.0 %collective-permute-start.6 = (bf16[256,512]{0,1:T(8,128)(2,1)}, bf16[256,512]{0,1:T(8,128)(2,1)S(1)}, u32[]{:S(2)}, u32[]{:S(2)}) collective-permute-start(bf16[256,512]{0,1:T(8,128)(2,1)} %copy.50), channel_id=1, source_target_pairs={{0,8},{2,10},{4,12},{6,14},{1,9},{3,11},{5,13},{7,15},{16,24},{18,... | collective-permute-start | bytes 786440 | tf_op jit(solution)/shard_map/ppermute | solution.py:36
  15.8 85.5 %collective-permute-start.4 = (bf16[256,512]{0,1:T(8,128)(2,1)}, bf16[256,512]{0,1:T(8,128)(2,1)S(1)}, u32[]{:S(2)}, u32[]{:S(2)}) collective-permute-start(bf16[256,512]{0,1:T(8,128)(2,1)} %copy.50), channel_id=1, source_target_pairs={{0,6},{2,8},{4,10},{6,12},{8,14},{1,7},{3,9},{5,11},{7,13},{9,15},... | collective-permute-start | bytes 786440 | tf_op jit(solution)/shard_map/ppermute | solution.py:36
  18.7 86.8 %collective-permute-start.2 = (bf16[256,512]{0,1:T(8,128)(2,1)}, bf16[256,512]{0,1:T(8,128)(2,1)}, u32[]{:S(2)}, u32[]{:S(2)}) collective-permute-start(bf16[256,512]{0,1:T(8,128)(2,1)} %copy.50), channel_id=1, source_target_pairs={{0,4},{2,6},{4,8},{6,10},{8,12},{10,14},{1,5},{3,7},{5,9},{7,11},{... | collective-permute-start | bytes 786440 | tf_op jit(solution)/shard_map/ppermute | solution.py:36
  21.3 39.0 %collective-permute-start.1 = (bf16[256,512]{1,0:T(8,128)(2,1)}, bf16[256,512]{1,0:T(8,128)(2,1)S(1)}, u32[]{:S(2)}, u32[]{:S(2)}) collective-permute-start(bf16[256,512]{1,0:T(8,128)(2,1)} %param.7), channel_id=1, source_target_pairs={{0,2},{2,4},{4,6},{6,8},{8,10},{10,12},{12,14},{1,3},{3,5},{5,7},{... | collective-permute-start | bytes 786440 | tf_op jit(solution)/shard_map/ppermute | solution.py:36
  60.3 51.7 %collective-permute-start = (bf16[256,512]{0,1:T(8,128)(2,1)}, bf16[256,512]{0,1:T(8,128)(2,1)}, u32[]{:S(2)}, u32[]{:S(2)}) collective-permute-start(bf16[256,512]{0,1:T(8,128)(2,1)} %copy.50), channel_id=1, source_target_pairs={{0,2},{2,4},{4,6},{6,8},{8,10},{10,12},{12,14},{1,3},{3,5},{5,7},{... | collective-permute-start | bytes 786440 | tf_op jit(solution)/shard_map/ppermute | solution.py:36
  82.3 157.4 %collective-permute-start.3 = (bf16[256,512]{1,0:T(8,128)(2,1)}, bf16[256,512]{1,0:T(8,128)(2,1)}, u32[]{:S(2)}, u32[]{:S(2)}) collective-permute-start(bf16[256,512]{1,0:T(8,128)(2,1)} %param.7), channel_id=1, source_target_pairs={{0,4},{2,6},{4,8},{6,10},{8,12},{10,14},{1,5},{3,7},{5,9},{7,11},{... | collective-permute-start | bytes 786440 | tf_op jit(solution)/shard_map/ppermute | solution.py:36
  97.0 92.0 %collective-permute-start.9 = (bf16[512,2048]{1,0:T(8,128)(2,1)}, bf16[512,2048]{1,0:T(8,128)(2,1)S(1)}, u32[]{:S(2)}, u32[]{:S(2)}) collective-permute-start(bf16[512,2048]{1,0:T(8,128)(2,1)} %collective-permute-done.8), channel_id=1, source_target_pairs={{0,2},{2,4},{4,6},{6,8},{8,10},{10,12},{12,14},{14,0},{1,3},{3,5},... | collective-permute-start | bytes 6291464 | tf_op jit(solution)/shard_map/ppermute | solution.py:24
  101.3 90.1 %copy-start = (f32[4,256,256,4]{2,1,3,0:T(8,128)}, f32[4,256,256,4]{2,1,3,0:T(8,128)S(1)}, u32[]{:S(2)}) copy-start(f32[4,256,256,4]{2,1,3,0:T(8,128)S(1)} %get-tuple-element.29) | copy-start | bytes 12582916
  101.3 139.5 %collective-permute-start.5 = (bf16[256,512]{1,0:T(8,128)(2,1)}, bf16[256,512]{1,0:T(8,128)(2,1)}, u32[]{:S(2)}, u32[]{:S(2)}) collective-permute-start(bf16[256,512]{1,0:T(8,128)(2,1)} %param.7), channel_id=1, source_target_pairs={{0,6},{2,8},{4,10},{6,12},{8,14},{1,7},{3,9},{5,11},{7,13},{9,15},... | collective-permute-start | bytes 786440 | tf_op jit(solution)/shard_map/ppermute | solution.py:36
  103.4 8.7 %copy-start.6 = (bf16[512,2048]{1,0:T(8,128)(2,1)S(1)}, bf16[512,2048]{1,0:T(8,128)(2,1)}, u32[]{:S(2)}) copy-start(bf16[512,2048]{1,0:T(8,128)(2,1)} %param.9) | copy-start | bytes 6291460
  105.5 8.8 %copy-start.2 = (f32[4,256,256,4]{2,1,3,0:T(8,128)}, f32[4,256,256,4]{2,1,3,0:T(8,128)S(1)}, u32[]{:S(2)}) copy-start(f32[4,256,256,4]{2,1,3,0:T(8,128)S(1)} %get-tuple-element.31) | copy-start | bytes 12582916
  105.5 136.4 %collective-permute-start.7 = (bf16[256,512]{1,0:T(8,128)(2,1)}, bf16[256,512]{1,0:T(8,128)(2,1)}, u32[]{:S(2)}, u32[]{:S(2)}) collective-permute-start(bf16[256,512]{1,0:T(8,128)(2,1)} %param.7), channel_id=1, source_target_pairs={{0,8},{2,10},{4,12},{6,14},{1,9},{3,11},{5,13},{7,15},{16,24},{18,... | collective-permute-start | bytes 786440 | tf_op jit(solution)/shard_map/ppermute | solution.py:36
  112.0 126.6 %copy-start.4 = (f32[4,256,256,4]{2,1,3,0:T(8,128)}, f32[4,256,256,4]{2,1,3,0:T(8,128)S(1)}, u32[]{:S(2)}) copy-start(f32[4,256,256,4]{2,1,3,0:T(8,128)S(1)} %get-tuple-element.33) | copy-start | bytes 12582916
  112.0 87.7 %collective-permute-start.12 = (bf16[512,2048]{1,0:T(8,128)(2,1)S(1)}, bf16[512,2048]{1,0:T(8,128)(2,1)}, u32[]{:S(2)}, u32[]{:S(2)}) collective-permute-start(bf16[512,2048]{1,0:T(8,128)(2,1)S(1)} %copy-done.6), channel_id=1, source_target_pairs={{2,0},{4,2},{6,4},{8,6},{10,8},{12,10},{14,12},{0,14},{3,1},{5,3},... | collective-permute-start | bytes 6291464 | tf_op jit(solution)/shard_map/ppermute | solution.py:26
  189.0 4.5 %copy-start.7 = (bf16[512,2048]{1,0:T(8,128)(2,1)}, bf16[512,2048]{1,0:T(8,128)(2,1)S(1)}, u32[]{:S(2)}) copy-start(bf16[512,2048]{1,0:T(8,128)(2,1)S(1)} %collective-permute-done.9) | copy-start | bytes 6291460
  189.0 48.0 %collective-permute-start.10 = (bf16[512,2048]{1,0:T(8,128)(2,1)S(1)}, bf16[512,2048]{1,0:T(8,128)(2,1)}, u32[]{:S(2)}, u32[]{:S(2)}) collective-permute-start(bf16[512,2048]{1,0:T(8,128)(2,1)S(1)} %collective-permute-done.9), channel_id=1, source_target_pairs={{0,2},{2,4},{4,6},{6,8},{8,10},{10,12},{12,14},{14,0},{1,3},{3,5},... | collective-permute-start | bytes 6291464 | tf_op jit(solution)/shard_map/ppermute | solution.py:24
  199.7 127.0 %collective-permute-start.13 = (bf16[512,2048]{1,0:T(8,128)(2,1)}, bf16[512,2048]{1,0:T(8,128)(2,1)}, u32[]{:S(2)}, u32[]{:S(2)}) collective-permute-start(bf16[512,2048]{1,0:T(8,128)(2,1)} %collective-permute-done.12), channel_id=1, source_target_pairs={{2,0},{4,2},{6,4},{8,6},{10,8},{12,10},{14,12},{0,14},{3,1},{5,3},... | collective-permute-start | bytes 6291464 | tf_op jit(solution)/shard_map/ppermute | solution.py:26
  237.0 95.0 %collective-permute-start.11 = (bf16[512,2048]{1,0:T(8,128)(2,1)}, bf16[512,2048]{1,0:T(8,128)(2,1)}, u32[]{:S(2)}, u32[]{:S(2)}) collective-permute-start(bf16[512,2048]{1,0:T(8,128)(2,1)} %collective-permute-done.10), channel_id=1, source_target_pairs={{0,2},{2,4},{4,6},{6,8},{8,10},{10,12},{12,14},{14,0},{1,3},{3,5},... | collective-permute-start | bytes 6291464 | tf_op jit(solution)/shard_map/ppermute | solution.py:24
  243.0 3.6 copy-start.3
  243.1 4.8 %copy-start.13 = (f32[4,4,256,128]{2,3,1,0:T(8,128)S(1)}, f32[4,4,256,128]{2,3,1,0:T(8,128)}, u32[]{:S(2)}) copy-start(f32[4,4,256,128]{2,3,1,0:T(8,128)} %fusion.21) | copy-start | bytes 6291460
  252.5 83.2 %copy-start.8 = (bf16[512,2048]{1,0:T(8,128)(2,1)S(1)}, bf16[512,2048]{1,0:T(8,128)(2,1)}, u32[]{:S(2)}) copy-start(bf16[512,2048]{1,0:T(8,128)(2,1)} %copy-done.7) | copy-start | bytes 6291460
  326.8 50.6 %collective-permute-start.14 = (bf16[512,2048]{1,0:T(8,128)(2,1)}, bf16[512,2048]{1,0:T(8,128)(2,1)S(1)}, u32[]{:S(2)}, u32[]{:S(2)}) collective-permute-start(bf16[512,2048]{1,0:T(8,128)(2,1)} %collective-permute-done.13), channel_id=1, source_target_pairs={{2,0},{4,2},{6,4},{8,6},{10,8},{12,10},{14,12},{0,14},{3,1},{5,3},... | collective-permute-start | bytes 6291464 | tf_op jit(solution)/shard_map/ppermute | solution.py:26
  (6 other events, 14.3 us)
Sparse Core Ops, SparseCore 0:
  252.6 44.7 all-gather.1
